TPU v7x, 128 devices: a whole 4x4x4 slice. The times are simulated.
128 devices in a mesh: dof: 32 (over x, z, core), snap: 4 (over y).
Axes of the slice: x: 4, y: 4, z: 4, core: 2. Of those that a mesh axis runs over, the one named last changes fastest.
Arguments:
- snapshots: bfloat16 [131072, 1024], P('dof', 'snap')
- lengths: int32 [16], replicated, may hold values from 16 to 64, as said below
- start_block: float32 [1024, 128], replicated, may hold values from -6 to 6
Outputs:
- pod_modes: float32 [131072, 128], P(('dof', 'snap'))
- r_factor: float32 [1024, 1024], replicated
Inputs may be any that keep to these rules, and one draw needn't show every extreme that they name: `lengths`: some passage has all 64 steps active and some passage only a quarter of them.
All inputs are finite; a program needn't handle non-finite values.
Results may differ from a plain program's by a relative error of at most 0.0003.
Values may be sent and summed in bfloat16 or wider, within the bound.
No kernel may reach another device: no remote copies, remote signals or barrier semaphores. Data moves between devices by JAX's collectives and lax.ppermute only.
A program may use at most 128 MiB of HBM per device.

v0:
```python
import jax
import jax.numpy as jnp
from jax import lax
from jax.sharding import PartitionSpec as P

STEPS = 64
ITERS = 3
PASSES = 16
TILE = 128


def pack_upper(rows):
    width = rows.shape[1]
    pieces = []
    for i in range(width // TILE):
        lhs = rows[:, i * TILE : (i + 1) * TILE]
        rhs = rows[:, i * TILE :]
        pieces.append(
            lax.dot_general(lhs, rhs, (((0,), (0,)), ((), ())), preferred_element_type=jnp.float32)
        )
    return jnp.concatenate(pieces, axis=1)


def unpack_upper(packed, width):
    blocks = width // TILE
    upper_rows = []
    offset = 0
    for i in range(blocks):
        w = width - i * TILE
        piece = packed[:, offset : offset + w]
        offset += w
        upper_rows.append(jnp.pad(piece, ((0, 0), (i * TILE, 0))))
    upper = jnp.concatenate(upper_rows, axis=0)
    r = lax.broadcasted_iota(jnp.int32, (width, width), 0) // TILE
    c = lax.broadcasted_iota(jnp.int32, (width, width), 1) // TILE
    return jnp.where(r <= c, upper, upper.T)


def body(snapshots, lengths, start_block):
    rows = lax.all_to_all(snapshots, "snap", 0, 1, tiled=True)
    width = rows.shape[1]
    col_length = jnp.repeat(lengths, STEPS, total_repeat_length=width)
    columns = jnp.arange(width, dtype=jnp.int32)
    active = columns % STEPS < col_length
    masked = jnp.where(active[None, :], rows, jnp.zeros_like(rows))
    row_count = snapshots.shape[0] * lax.axis_size("dof")
    packed = lax.psum(pack_upper(masked), ("dof", "snap"))
    gram_sum = unpack_upper(packed, width)
    shifted = gram_sum / jnp.float32(row_count) + 0.05 * jnp.eye(width, dtype=jnp.float32)
    upper_factor = lax.linalg.cholesky(shifted, symmetrize_input=False).T
    contract = (((0,), (0,)), ((), ()))
    subspace = start_block
    for sweep in range(ITERS):
        image = jnp.dot(
            shifted, subspace, precision=lax.Precision.HIGHEST, preferred_element_type=jnp.float32
        )
        correlation = lax.dot_general(
            image,
            image,
            contract,
            precision=lax.Precision.HIGHEST,
            preferred_element_type=jnp.float32,
        )
        lower_factor = jnp.linalg.cholesky(correlation)
        subspace = lax.linalg.triangular_solve(
            lower_factor, image, left_side=False, lower=True, transpose_a=True
        )
    pod_modes = jnp.dot(
        masked.astype(jnp.float32),
        subspace,
        precision=lax.Precision.HIGHEST,
        preferred_element_type=jnp.float32,
    )
    return (pod_modes, upper_factor)


def solution(mesh):
    placed = (P("dof", "snap"), P(), P())
    return jax.shard_map(
        body, mesh=mesh, in_specs=placed, out_specs=(P(("dof", "snap"), None), P()), check_vma=False
    )
```

profile of v0, /device:TPU:1, one launch (start us, length us, event | category | flops | bytes accessed | tf_op | source)
XLA Modules:
  0.0 540.3 jit_solution(2373709611297239090)
XLA Ops:
  7.2 5.2 all-to-all-start
  13.2 4.4 compare_select_fusion.1
  17.7 5.7 %fusion.98 = pred[1024]{0:T(1024)(128)(4,1)S(1)} fusion(pred[1024]{0:T(1024)(128)(4,1)S(1)} %get-tuple-element.30, pred[1024]{0:T(1024)(128)(4,1)S(1)} %get-tuple-element.29, pred[1024]{0:T(1024)(128)(4,1)S(1)} %get-tuple-element.28, pred[1024]{0:T(1024)(128)(4,1)S(1)} %get-tuple-element.27, pred[1024]{0:T(1024)(128)(4,1)S(1)} %get-tuple-element.26, ...), kind=kLoop, calls=%fused_computation.159 | loop fusion | flops 25600 | bytes 18500 | tf_op jit(solution)/shard_map/lt | solution.py:44
  23.4 14.4 %all-to-all-done = bf16[4,1024,256]{2,1,0:T(8,128)(2,1)S(1)} async-done(((bf16[4,1024,256]{2,1,0:T(8,128)(2,1)}), bf16[4,1024,256]{2,1,0:T(8,128)(2,1)S(1)}, u32[]{:S(2)}, u32[]{:S(2)}) %all-to-all-start) | async-done | bytes 2097184 | tf_op jit(solution)/shard_map/all_to_all | solution.py:40
  37.8 2.4 copy.29
  40.1 1.8 bitcast_select_fusion.1
  42.0 1.5 convolution_dynamic-update-slice_fusion
  43.5 1.4 fusion.8
  44.9 1.3 fusion.11
  46.2 1.2 fusion.14
  47.4 1.1 convolution_dynamic-update-slice_fusion.4
  48.6 1.0 convolution_dynamic-update-slice_fusion.6
  49.6 1.0 convolution_dynamic-update-slice_fusion.7
  51.5 152.8 %all-reduce.10.cloned.1.call-done = f32[128,4608]{0,1:T(8,128)} async-done(((f32[128,4608]{0,1:T(8,128)}), f32[128,4608]{0,1:T(8,128)}) %all-reduce.10.cloned.1.call-update) | async-done | bytes 2359312 | tf_op jit(solution)/shard_map/psum | solution.py:47
  204.3 1.1 slice.269
  205.4 1.9 slice_dynamic-update-slice_fusion
  208.1 1.0 slice.270
  214.1 5.3 copy.37
  219.5 4.2 fusion.1
  223.7 2.0 copy-done.1
  225.7 11.7 %cholesky.247 = f32[128,128]{1,0:T(8,128)S(1)} custom-call(f32[128,128]{1,0:T(8,128)S(1)} %cholesky.667), custom_call_target="Cholesky" | custom-call | tf_op jit(solution)/shard_map/cholesky | solution.py:50
  238.1 9.8 %custom-call.49 = f32[1,128,128]{1,2,0:T(8,128)S(1)} custom-call(f32[1,128,128]{2,1,0:T(8,128)S(1)} %get-tuple-element.54), custom_call_target="InvertDiagBlocksLowerTriangular" | custom-call | tf_op jit(solution)/shard_map/cholesky | solution.py:50
  247.9 5.4 fusion.106
  253.3 1.0 fusion.107
  254.5 11.7 %cholesky.636 = f32[128,128]{1,0:T(8,128)S(1)} custom-call(f32[128,128]{1,0:T(8,128)S(1)} %fusion.63), custom_call_target="Cholesky" | custom-call | tf_op jit(solution)/shard_map/jit(cholesky)/cholesky | solution.py:64
  267.5 9.8 %custom-call.58 = f32[1,128,128]{1,2,0:T(8,128)S(1)} custom-call(f32[1,128,128]{2,1,0:T(8,128)S(1)} %fusion.46), custom_call_target="InvertDiagBlocksLowerTriangular" | custom-call | tf_op jit(solution)/shard_map/triangular_solve/custom-call.16 | solution.py:65
  278.0 5.4 %fusion.108 = f32[1024,128]{1,0:T(8,128)S(1)} fusion(f32[1024,1024]{1,0:T(8,128)} %copy-done.1, f32[1024,128]{0,1:T(8,128)S(1)} %convolution_bitcast_fusion.2), kind=kOutput, calls=%fused_computation.192 | convolution fusion | flops 1610612736 | bytes 5242880 | tf_op jit(solution)/shard_map/dot_general | solution.py:54
  283.4 1.0 fusion.109
  284.6 11.7 %cholesky.647 = f32[128,128]{1,0:T(8,128)S(1)} custom-call(f32[128,128]{1,0:T(8,128)S(1)} %fusion.61), custom_call_target="Cholesky" | custom-call | tf_op jit(solution)/shard_map/jit(cholesky)/cholesky | solution.py:64
  297.6 9.8 %custom-call.59 = f32[1,128,128]{1,2,0:T(8,128)S(1)} custom-call(f32[1,128,128]{2,1,0:T(8,128)S(1)} %fusion.47), custom_call_target="InvertDiagBlocksLowerTriangular" | custom-call | tf_op jit(solution)/shard_map/triangular_solve/custom-call.16 | solution.py:65
  308.1 5.6 %fusion.110 = f32[1024,128]{1,0:T(8,128)S(1)} fusion(f32[1024,1024]{1,0:T(8,128)} %copy-done.1, f32[1024,128]{0,1:T(8,128)S(1)} %convolution_bitcast_fusion.1), kind=kOutput, calls=%fused_computation.194 | convolution fusion | flops 1610612736 | bytes 5242880 | tf_op jit(solution)/shard_map/dot_general | solution.py:54
  313.7 1.0 fusion.111
  314.8 11.7 %cholesky.658 = f32[128,128]{1,0:T(8,128)S(1)} custom-call(f32[128,128]{1,0:T(8,128)S(1)} %fusion.59), custom_call_target="Cholesky" | custom-call | tf_op jit(solution)/shard_map/jit(cholesky)/cholesky | solution.py:64
  327.9 9.8 %custom-call.60 = f32[1,128,128]{1,2,0:T(8,128)S(1)} custom-call(f32[1,128,128]{2,1,0:T(8,128)S(1)} %fusion.48), custom_call_target="InvertDiagBlocksLowerTriangular" | custom-call | tf_op jit(solution)/shard_map/triangular_solve/custom-call.16 | solution.py:65
  338.4 3.1 fusion.112
  341.5 2.5 cholesky.279
  343.9 2.4 constant_dynamic-update-slice_fusion.6
  346.3 1.5 convolution_subtract_fusion
  347.9 11.9 %cholesky.270 = f32[128,128]{1,0:T(8,128)S(1)} custom-call(f32[128,128]{1,0:T(8,128)S(1)} %cholesky.671), custom_call_target="Cholesky" | custom-call | tf_op jit(solution)/shard_map/cholesky | solution.py:50
  361.1 9.8 %custom-call.50 = f32[1,128,128]{1,2,0:T(8,128)S(1)} custom-call(f32[1,128,128]{2,1,0:T(8,128)S(1)} %get-tuple-element.51), custom_call_target="InvertDiagBlocksLowerTriangular" | custom-call | tf_op jit(solution)/shard_map/cholesky | solution.py:50
  370.9 1.3 convolution_dynamic-update-slice_fusion.1
  372.2 2.1 convolution_subtract_fusion.1
  374.3 11.7 %cholesky.493 = f32[128,128]{1,0:T(8,128)S(1)} custom-call(f32[128,128]{1,0:T(8,128)S(1)} %cholesky.676), custom_call_target="Cholesky" | custom-call | tf_op jit(solution)/shard_map/cholesky | solution.py:50
  387.3 10.0 %custom-call.51 = f32[1,128,128]{1,2,0:T(8,128)S(1)} custom-call(f32[1,128,128]{2,1,0:T(8,128)S(1)} %get-tuple-element.48), custom_call_target="InvertDiagBlocksLowerTriangular" | custom-call | tf_op jit(solution)/shard_map/cholesky | solution.py:50
  397.4 1.2 convolution_dynamic-update-slice_fusion.2
  398.5 2.3 convolution_subtract_fusion.2
  400.9 11.7 %cholesky.512 = f32[128,128]{1,0:T(8,128)S(1)} custom-call(f32[128,128]{1,0:T(8,128)S(1)} %cholesky.681), custom_call_target="Cholesky" | custom-call | tf_op jit(solution)/shard_map/cholesky | solution.py:50
  413.9 9.8 %custom-call.52 = f32[1,128,128]{1,2,0:T(8,128)S(1)} custom-call(f32[1,128,128]{2,1,0:T(8,128)S(1)} %get-tuple-element.45), custom_call_target="InvertDiagBlocksLowerTriangular" | custom-call | tf_op jit(solution)/shard_map/cholesky | solution.py:50
  423.7 1.1 convolution_dynamic-update-slice_fusion.3
  424.8 2.3 convolution_subtract_fusion.3
  427.1 12.1 %cholesky.531 = f32[128,128]{1,0:T(8,128)S(1)} custom-call(f32[128,128]{1,0:T(8,128)S(1)} %cholesky.686), custom_call_target="Cholesky" | custom-call | tf_op jit(solution)/shard_map/cholesky | solution.py:50
  440.5 9.8 %custom-call.53 = f32[1,128,128]{1,2,0:T(8,128)S(1)} custom-call(f32[1,128,128]{2,1,0:T(8,128)S(1)} %get-tuple-element.42), custom_call_target="InvertDiagBlocksLowerTriangular" | custom-call | tf_op jit(solution)/shard_map/cholesky | solution.py:50
  450.3 1.0 convolution_dynamic-update-slice_fusion.5
  451.3 2.3 convolution_subtract_fusion.4
  453.6 11.7 %cholesky.551 = f32[128,128]{1,0:T(8,128)S(1)} custom-call(f32[128,128]{1,0:T(8,128)S(1)} %cholesky.691), custom_call_target="Cholesky" | custom-call | tf_op jit(solution)/shard_map/cholesky | solution.py:50
  466.7 9.8 %custom-call.54 = f32[1,128,128]{1,2,0:T(8,128)S(1)} custom-call(f32[1,128,128]{2,1,0:T(8,128)S(1)} %get-tuple-element.39), custom_call_target="InvertDiagBlocksLowerTriangular" | custom-call | tf_op jit(solution)/shard_map/cholesky | solution.py:50
  476.5 0.9 convolution_dynamic-update-slice_fusion.8
  477.4 2.0 convolution_subtract_fusion.5
  479.5 11.9 %cholesky.571 = f32[128,128]{1,0:T(8,128)S(1)} custom-call(f32[128,128]{1,0:T(8,128)S(1)} %cholesky.696), custom_call_target="Cholesky" | custom-call | tf_op jit(solution)/shard_map/cholesky | solution.py:50
  492.6 9.8 %custom-call.55 = f32[1,128,128]{1,2,0:T(8,128)S(1)} custom-call(f32[1,128,128]{2,1,0:T(8,128)S(1)} %get-tuple-element.36), custom_call_target="InvertDiagBlocksLowerTriangular" | custom-call | tf_op jit(solution)/shard_map/cholesky | solution.py:50
  503.3 1.8 convolution_subtract_fusion.6
  505.1 11.7 %cholesky.589 = f32[128,128]{1,0:T(8,128)S(1)} custom-call(f32[128,128]{1,0:T(8,128)S(1)} %convolution_subtract_fusion.6), custom_call_target="Cholesky" | custom-call | tf_op jit(solution)/shard_map/cholesky | solution.py:50
  523.1 4.8 select_bitcast_fusion
  527.9 5.3 copy.41
  (75 shorter events, 24.6 us)
Async XLA Ops:
  7.2 240.8 %copy-start = (f32[1024,128]{1,0:T(8,128)S(1)}, f32[1024,128]{1,0:T(8,128)}, u32[]{:S(2)}) copy-start(f32[1024,128]{1,0:T(8,128)} %param.10) | copy-start | bytes 1572868
  7.2 5.9 %copy-start.3 = (s32[8,128]{1,0:T(8,128)S(1)}, s32[8,128]{1,0:T(8,128)}, u32[]{:S(2)}) copy-start(s32[8,128]{1,0:T(8,128)} %constant.336.clone.1) | copy-start | bytes 12292
  7.2 5.2 copy-start.2
  7.2 30.6 %all-to-all-start = ((bf16[4,1024,256]{2,1,0:T(8,128)(2,1)}), bf16[4,1024,256]{2,1,0:T(8,128)(2,1)S(1)}, u32[]{:S(2)}, u32[]{:S(2)}) async-start(bf16[4,1024,256]{2,1,0:T(8,128)(2,1)} %bitcast.129), calls=%async_computation | async-start | bytes 4194304 | tf_op jit(solution)/shard_map/all_to_all | solution.py:40
  12.4 191.9 %all-reduce.10.cloned.1.call-start = ((), (), s32[]{:S(2)}) async-start(), calls=%async_computation.1 | async-start | bytes 4718592 | tf_op jit(solution)/shard_map/psum | solution.py:47
  204.3 5.7 %slice-start = ((f32[128,4608]{0,1:T(8,128)}), f32[128,640]{0,1:T(8,128)S(1)}, s32[]{:S(2)}) async-start(f32[128,4608]{0,1:T(8,128)} %all-reduce.10.cloned.1.call-done), calls=%async_computation.2 | async-start | bytes 655360 | tf_op jit(solution)/shard_map/slice | solution.py:30
  204.3 6.6 %slice-start.1 = ((f32[128,4608]{0,1:T(8,128)}), f32[128,512]{0,1:T(8,128)S(1)}, s32[]{:S(2)}) async-start(f32[128,4608]{0,1:T(8,128)} %all-reduce.10.cloned.1.call-done), calls=%async_computation.3 | async-start | bytes 524288 | tf_op jit(solution)/shard_map/slice | solution.py:30
  204.3 7.4 %slice-start.2 = ((f32[128,4608]{0,1:T(8,128)}), f32[128,384]{0,1:T(8,128)S(1)}, s32[]{:S(2)}) async-start(f32[128,4608]{0,1:T(8,128)} %all-reduce.10.cloned.1.call-done), calls=%async_computation.4 | async-start | bytes 393216 | tf_op jit(solution)/shard_map/slice | solution.py:30
  205.4 7.1 %slice-start.3 = ((f32[128,4608]{0,1:T(8,128)}), f32[128,256]{0,1:T(8,128)S(1)}, s32[]{:S(2)}) async-start(f32[128,4608]{0,1:T(8,128)} %all-reduce.10.cloned.1.call-done), calls=%async_computation.5 | async-start | bytes 262144 | tf_op jit(solution)/shard_map/slice | solution.py:30
  205.4 7.9 %slice-start.4 = ((f32[128,4608]{0,1:T(8,128)}), f32[128,128]{0,1:T(8,128)S(1)}, s32[]{:S(2)}) async-start(f32[128,4608]{0,1:T(8,128)} %all-reduce.10.cloned.1.call-done), calls=%async_computation.6 | async-start | bytes 131072 | tf_op jit(solution)/shard_map/slice | solution.py:30
  223.7 2.0 copy-start.1
Sparse Core Ops, SparseCore 0:
  51.6 152.6 all-reduce.9
where the time goes:
time: 549 us; the launch traced here: 540 us
  other arithmetic  263 us (48%)
  waiting for transfers between devices  167 us (30%)
  matrix products  57.1 us (10%)
  local copies, waits for them, and re-layouts  28.4 us (5%)
  between operations  19.6 us (4%)
    another operation x31, other arithmetic, body(): upper_factor = lax.linalg.cholesky(shifted, symmetrize_input=False).T  173 us
    psum x1, waiting for transfers between devices, body(): packed = lax.psum(pack_upper(masked), ('dof', 'snap'))  153 us
    another operation x9, other arithmetic, body(): lower_factor = jnp.linalg.cholesky(correlation)  37.2 us
    another operation x6, other arithmetic, body(): lax.linalg.triangular_solve(lower_factor, image, left_side=False, lower=T...  31.4 us
    another operation x14, matrix products, body(): upper_factor = lax.linalg.cholesky(shifted, symmetrize_input=False).T  23.1 us
    dot_general x3, matrix products, body(): jnp.dot(shifted, subspace, precision=lax.Precision.HIGHEST, preferred_ele...  16.4 us
    all_to_all x1, waiting for transfers between devices, body(): rows = lax.all_to_all(snapshots, 'snap', 0, 1, tiled=True)  14.4 us
    unnamed x16, local copies, waits for them, and re-layouts  14.2 us
  transfers between devices with their start and end apart: 2, of which 2 were waited for; matrix products, arithmetic and copies ran while one was open for 2% of the time, Pallas kernels for 0%

commit v1 on v0

--- a/solution.py
+++ b/solution.py
@@ -44,7 +44,8 @@
     active = columns % STEPS < col_length
     masked = jnp.where(active[None, :], rows, jnp.zeros_like(rows))
     row_count = snapshots.shape[0] * lax.axis_size("dof")
-    packed = lax.psum(pack_upper(masked), ("dof", "snap"))
+    partial = lax.psum(pack_upper(masked), "snap")
+    packed = lax.psum(partial, "dof")
     gram_sum = unpack_upper(packed, width)
     shifted = gram_sum / jnp.float32(row_count) + 0.05 * jnp.eye(width, dtype=jnp.float32)
     upper_factor = lax.linalg.cholesky(shifted, symmetrize_input=False).T

time: 549 us -> 567 us (1.033)
  waiting for transfers between devices: 167 us -> 190 us
    psum x1 -> x2, waiting for transfers between devices: 153 us -> 175 us  [the longest x1 111 us: body(): packed = lax.psum(partial, 'dof')]
  transfers between devices with their start and end apart: 2 -> 3, of which waited for: 2 -> 3; matrix products, arithmetic and copies ran while one was open for 2% -> 2% of each run, Pallas kernels for 0% -> 0%
where the time goes in v1:
time: 567 us; the launch traced here: 563 us
  other arithmetic  263 us (46%)
  waiting for transfers between devices  190 us (34%)
  matrix products  57.1 us (10%)
  local copies, waits for them, and re-layouts  28.4 us (5%)
  between operations  19.7 us (3%)
    another operation x31, other arithmetic, body(): upper_factor = lax.linalg.cholesky(shifted, symmetrize_input=False).T  173 us
    psum x1, waiting for transfers between devices, body(): packed = lax.psum(partial, 'dof')  111 us
    psum x1, waiting for transfers between devices, body(): partial = lax.psum(pack_upper(masked), 'snap')  64.5 us
    another operation x9, other arithmetic, body(): lower_factor = jnp.linalg.cholesky(correlation)  37.2 us
    another operation x6, other arithmetic, body(): lax.linalg.triangular_solve(lower_factor, image, left_side=False, lower=T...  31.4 us
    another operation x14, matrix products, body(): upper_factor = lax.linalg.cholesky(shifted, symmetrize_input=False).T  23.2 us
    dot_general x3, matrix products, body(): jnp.dot(shifted, subspace, precision=lax.Precision.HIGHEST, preferred_ele...  16.4 us
    all_to_all x1, waiting for transfers between devices, body(): rows = lax.all_to_all(snapshots, 'snap', 0, 1, tiled=True)  14.4 us
  transfers between devices with their start and end apart: 3, of which 3 were waited for; matrix products, arithmetic and copies ran while one was open for 2% of the time, Pallas kernels for 0%

profile of v1, /device:TPU:1, one launch (start us, length us, event | category | flops | bytes accessed | tf_op | source)
XLA Modules:
  0.0 563.0 jit_solution(17462333356909838093)
XLA Ops:
  7.2 5.2 all-to-all-start
  13.2 4.4 compare_select_fusion.1
  17.7 5.7 %fusion.98 = pred[1024]{0:T(1024)(128)(4,1)S(1)} fusion(pred[1024]{0:T(1024)(128)(4,1)S(1)} %get-tuple-element.30, pred[1024]{0:T(1024)(128)(4,1)S(1)} %get-tuple-element.29, pred[1024]{0:T(1024)(128)(4,1)S(1)} %get-tuple-element.28, pred[1024]{0:T(1024)(128)(4,1)S(1)} %get-tuple-element.27, pred[1024]{0:T(1024)(128)(4,1)S(1)} %get-tuple-element.26, ...), kind=kLoop, calls=%fused_computation.159 | loop fusion | flops 25600 | bytes 18500 | tf_op jit(solution)/shard_map/lt | solution.py:44
  23.4 14.4 %all-to-all-done = bf16[4,1024,256]{2,1,0:T(8,128)(2,1)S(1)} async-done(((bf16[4,1024,256]{2,1,0:T(8,128)(2,1)}), bf16[4,1024,256]{2,1,0:T(8,128)(2,1)S(1)}, u32[]{:S(2)}, u32[]{:S(2)}) %all-to-all-start) | async-done | bytes 2097184 | tf_op jit(solution)/shard_map/all_to_all | solution.py:40
  37.8 2.4 copy.29
  40.1 1.8 bitcast_select_fusion.1
  42.0 1.5 convolution_dynamic-update-slice_fusion
  43.5 1.4 fusion.8
  44.9 1.3 fusion.11
  46.2 1.2 fusion.14
  47.4 1.1 convolution_dynamic-update-slice_fusion.4
  48.6 1.0 convolution_dynamic-update-slice_fusion.6
  49.6 1.0 convolution_dynamic-update-slice_fusion.7
  51.7 64.5 %all-reduce.11.cloned.1.call-done = f32[128,4608]{0,1:T(8,128)} async-done(((f32[128,4608]{0,1:T(8,128)}), f32[128,4608]{0,1:T(8,128)}) %all-reduce.11.cloned.1.call-update) | async-done | bytes 2359312 | tf_op jit(solution)/shard_map/psum | solution.py:47
  116.2 110.7 %all-reduce.13.cloned.1.call-done = f32[128,4608]{0,1:T(8,128)} async-done(((f32[128,4608]{0,1:T(8,128)}), f32[128,4608]{0,1:T(8,128)}) %all-reduce.13.cloned.1.call-update) | async-done | bytes 2359312 | tf_op jit(solution)/shard_map/psum | solution.py:48
  226.9 1.1 slice.269
  228.1 1.9 slice_dynamic-update-slice_fusion
  230.8 1.0 slice.270
  236.8 5.3 copy.37
  242.2 4.2 fusion.1
  246.4 2.0 copy-done.1
  248.4 11.7 %cholesky.247 = f32[128,128]{1,0:T(8,128)S(1)} custom-call(f32[128,128]{1,0:T(8,128)S(1)} %cholesky.667), custom_call_target="Cholesky" | custom-call | tf_op jit(solution)/shard_map/cholesky | solution.py:51
  260.8 9.8 %custom-call.49 = f32[1,128,128]{1,2,0:T(8,128)S(1)} custom-call(f32[1,128,128]{2,1,0:T(8,128)S(1)} %get-tuple-element.54), custom_call_target="InvertDiagBlocksLowerTriangular" | custom-call | tf_op jit(solution)/shard_map/cholesky | solution.py:51
  270.6 5.4 fusion.106
  276.0 1.0 fusion.107
  277.2 11.7 %cholesky.636 = f32[128,128]{1,0:T(8,128)S(1)} custom-call(f32[128,128]{1,0:T(8,128)S(1)} %fusion.63), custom_call_target="Cholesky" | custom-call | tf_op jit(solution)/shard_map/jit(cholesky)/cholesky | solution.py:65
  290.2 9.8 %custom-call.58 = f32[1,128,128]{1,2,0:T(8,128)S(1)} custom-call(f32[1,128,128]{2,1,0:T(8,128)S(1)} %fusion.46), custom_call_target="InvertDiagBlocksLowerTriangular" | custom-call | tf_op jit(solution)/shard_map/triangular_solve/custom-call.16 | solution.py:66
  300.7 5.6 fusion.108
  306.3 1.0 fusion.109
  307.5 11.7 %cholesky.647 = f32[128,128]{1,0:T(8,128)S(1)} custom-call(f32[128,128]{1,0:T(8,128)S(1)} %fusion.61), custom_call_target="Cholesky" | custom-call | tf_op jit(solution)/shard_map/jit(cholesky)/cholesky | solution.py:65
  320.5 9.8 %custom-call.59 = f32[1,128,128]{1,2,0:T(8,128)S(1)} custom-call(f32[1,128,128]{2,1,0:T(8,128)S(1)} %fusion.47), custom_call_target="InvertDiagBlocksLowerTriangular" | custom-call | tf_op jit(solution)/shard_map/triangular_solve/custom-call.16 | solution.py:66
  331.0 5.4 fusion.110
  336.4 1.0 fusion.111
  337.5 11.7 %cholesky.658 = f32[128,128]{1,0:T(8,128)S(1)} custom-call(f32[128,128]{1,0:T(8,128)S(1)} %fusion.59), custom_call_target="Cholesky" | custom-call | tf_op jit(solution)/shard_map/jit(cholesky)/cholesky | solution.py:65
  350.6 9.8 %custom-call.60 = f32[1,128,128]{1,2,0:T(8,128)S(1)} custom-call(f32[1,128,128]{2,1,0:T(8,128)S(1)} %fusion.48), custom_call_target="InvertDiagBlocksLowerTriangular" | custom-call | tf_op jit(solution)/shard_map/triangular_solve/custom-call.16 | solution.py:66
  361.0 3.1 fusion.112
  364.1 2.5 cholesky.279
  366.6 2.4 constant_dynamic-update-slice_fusion.6
  369.0 1.5 convolution_subtract_fusion
  370.6 11.9 %cholesky.270 = f32[128,128]{1,0:T(8,128)S(1)} custom-call(f32[128,128]{1,0:T(8,128)S(1)} %cholesky.671), custom_call_target="Cholesky" | custom-call | tf_op jit(solution)/shard_map/cholesky | solution.py:51
  383.8 9.8 %custom-call.50 = f32[1,128,128]{1,2,0:T(8,128)S(1)} custom-call(f32[1,128,128]{2,1,0:T(8,128)S(1)} %get-tuple-element.51), custom_call_target="InvertDiagBlocksLowerTriangular" | custom-call | tf_op jit(solution)/shard_map/cholesky | solution.py:51
  393.6 1.3 convolution_dynamic-update-slice_fusion.1
  394.9 2.1 convolution_subtract_fusion.1
  397.0 11.7 %cholesky.493 = f32[128,128]{1,0:T(8,128)S(1)} custom-call(f32[128,128]{1,0:T(8,128)S(1)} %cholesky.676), custom_call_target="Cholesky" | custom-call | tf_op jit(solution)/shard_map/cholesky | solution.py:51
  410.1 10.2 %custom-call.51 = f32[1,128,128]{1,2,0:T(8,128)S(1)} custom-call(f32[1,128,128]{2,1,0:T(8,128)S(1)} %get-tuple-element.48), custom_call_target="InvertDiagBlocksLowerTriangular" | custom-call | tf_op jit(solution)/shard_map/cholesky | solution.py:51
  420.3 1.2 convolution_dynamic-update-slice_fusion.2
  421.4 2.3 convolution_subtract_fusion.2
  423.8 11.7 %cholesky.512 = f32[128,128]{1,0:T(8,128)S(1)} custom-call(f32[128,128]{1,0:T(8,128)S(1)} %cholesky.681), custom_call_target="Cholesky" | custom-call | tf_op jit(solution)/shard_map/cholesky | solution.py:51
  436.8 9.8 %custom-call.52 = f32[1,128,128]{1,2,0:T(8,128)S(1)} custom-call(f32[1,128,128]{2,1,0:T(8,128)S(1)} %get-tuple-element.45), custom_call_target="InvertDiagBlocksLowerTriangular" | custom-call | tf_op jit(solution)/shard_map/cholesky | solution.py:51
  446.6 1.1 convolution_dynamic-update-slice_fusion.3
  447.7 2.3 convolution_subtract_fusion.3
  450.0 11.8 %cholesky.531 = f32[128,128]{1,0:T(8,128)S(1)} custom-call(f32[128,128]{1,0:T(8,128)S(1)} %cholesky.686), custom_call_target="Cholesky" | custom-call | tf_op jit(solution)/shard_map/cholesky | solution.py:51
  463.1 9.8 %custom-call.53 = f32[1,128,128]{1,2,0:T(8,128)S(1)} custom-call(f32[1,128,128]{2,1,0:T(8,128)S(1)} %get-tuple-element.42), custom_call_target="InvertDiagBlocksLowerTriangular" | custom-call | tf_op jit(solution)/shard_map/cholesky | solution.py:51
  473.0 1.0 convolution_dynamic-update-slice_fusion.5
  474.0 2.3 convolution_subtract_fusion.4
  476.3 11.7 %cholesky.551 = f32[128,128]{1,0:T(8,128)S(1)} custom-call(f32[128,128]{1,0:T(8,128)S(1)} %cholesky.691), custom_call_target="Cholesky" | custom-call | tf_op jit(solution)/shard_map/cholesky | solution.py:51
  489.3 9.8 %custom-call.54 = f32[1,128,128]{1,2,0:T(8,128)S(1)} custom-call(f32[1,128,128]{2,1,0:T(8,128)S(1)} %get-tuple-element.39), custom_call_target="InvertDiagBlocksLowerTriangular" | custom-call | tf_op jit(solution)/shard_map/cholesky | solution.py:51
  500.1 2.0 convolution_subtract_fusion.5
  502.1 11.9 %cholesky.571 = f32[128,128]{1,0:T(8,128)S(1)} custom-call(f32[128,128]{1,0:T(8,128)S(1)} %cholesky.696), custom_call_target="Cholesky" | custom-call | tf_op jit(solution)/shard_map/cholesky | solution.py:51
  515.4 9.8 %custom-call.55 = f32[1,128,128]{1,2,0:T(8,128)S(1)} custom-call(f32[1,128,128]{2,1,0:T(8,128)S(1)} %get-tuple-element.36), custom_call_target="InvertDiagBlocksLowerTriangular" | custom-call | tf_op jit(solution)/shard_map/cholesky | solution.py:51
  526.0 1.8 convolution_subtract_fusion.6
  527.8 11.7 %cholesky.589 = f32[128,128]{1,0:T(8,128)S(1)} custom-call(f32[128,128]{1,0:T(8,128)S(1)} %convolution_subtract_fusion.6), custom_call_target="Cholesky" | custom-call | tf_op jit(solution)/shard_map/cholesky | solution.py:51
  545.8 4.8 select_bitcast_fusion
  550.6 5.3 copy.41
  (78 shorter events, 25.8 us)
Async XLA Ops:
  7.2 263.4 %copy-start = (f32[1024,128]{1,0:T(8,128)S(1)}, f32[1024,128]{1,0:T(8,128)}, u32[]{:S(2)}) copy-start(f32[1024,128]{1,0:T(8,128)} %param.10) | copy-start | bytes 1572868
  7.2 5.9 %copy-start.3 = (s32[8,128]{1,0:T(8,128)S(1)}, s32[8,128]{1,0:T(8,128)}, u32[]{:S(2)}) copy-start(s32[8,128]{1,0:T(8,128)} %constant.336.clone.1) | copy-start | bytes 12292
  7.2 5.2 copy-start.2
  7.2 30.6 %all-to-all-start = ((bf16[4,1024,256]{2,1,0:T(8,128)(2,1)}), bf16[4,1024,256]{2,1,0:T(8,128)(2,1)S(1)}, u32[]{:S(2)}, u32[]{:S(2)}) async-start(bf16[4,1024,256]{2,1,0:T(8,128)(2,1)} %bitcast.129), calls=%async_computation | async-start | bytes 4194304 | tf_op jit(solution)/shard_map/all_to_all | solution.py:40
  12.4 103.8 %all-reduce.11.cloned.1.call-start = ((), (), s32[]{:S(2)}) async-start(), calls=%async_computation.1 | async-start | bytes 4718592 | tf_op jit(solution)/shard_map/psum | solution.py:47
  51.4 175.5 %all-reduce.13.cloned.1.call-start = ((), (), s32[]{:S(2)}) async-start(), calls=%async_computation.2 | async-start | bytes 4718592 | tf_op jit(solution)/shard_map/psum | solution.py:48
  226.9 5.7 %slice-start = ((f32[128,4608]{0,1:T(8,128)}), f32[128,640]{0,1:T(8,128)S(1)}, s32[]{:S(2)}) async-start(f32[128,4608]{0,1:T(8,128)} %all-reduce.13.cloned.1.call-done), calls=%async_computation.3 | async-start | bytes 655360 | tf_op jit(solution)/shard_map/slice | solution.py:30
  226.9 6.6 %slice-start.1 = ((f32[128,4608]{0,1:T(8,128)}), f32[128,512]{0,1:T(8,128)S(1)}, s32[]{:S(2)}) async-start(f32[128,4608]{0,1:T(8,128)} %all-reduce.13.cloned.1.call-done), calls=%async_computation.4 | async-start | bytes 524288 | tf_op jit(solution)/shard_map/slice | solution.py:30
  226.9 7.4 %slice-start.2 = ((f32[128,4608]{0,1:T(8,128)}), f32[128,384]{0,1:T(8,128)S(1)}, s32[]{:S(2)}) async-start(f32[128,4608]{0,1:T(8,128)} %all-reduce.13.cloned.1.call-done), calls=%async_computation.5 | async-start | bytes 393216 | tf_op jit(solution)/shard_map/slice | solution.py:30
  228.1 7.1 %slice-start.3 = ((f32[128,4608]{0,1:T(8,128)}), f32[128,256]{0,1:T(8,128)S(1)}, s32[]{:S(2)}) async-start(f32[128,4608]{0,1:T(8,128)} %all-reduce.13.cloned.1.call-done), calls=%async_computation.6 | async-start | bytes 262144 | tf_op jit(solution)/shard_map/slice | solution.py:30
  228.1 7.9 %slice-start.4 = ((f32[128,4608]{0,1:T(8,128)}), f32[128,128]{0,1:T(8,128)S(1)}, s32[]{:S(2)}) async-start(f32[128,4608]{0,1:T(8,128)} %all-reduce.13.cloned.1.call-done), calls=%async_computation.7 | async-start | bytes 131072 | tf_op jit(solution)/shard_map/slice | solution.py:30
  246.4 2.0 copy-start.1
Sparse Core Ops, SparseCore 0:
  51.6 64.5 all-reduce.10
  119.5 107.4 all-reduce.12
